TPU v7x, 512 devices: a whole 4x4x16 slice. The times are simulated.
512 devices in a mesh: grp: 4 (over x), ch: 128 (over y, z, core).
Axes of the slice: x: 4, y: 4, z: 16, core: 2. Of those that a mesh axis runs over, the one named last changes fastest.
Arguments:
- raw_strain: bfloat16 [4, 7680, 8192], P('grp', 'ch'), may hold values from -6 to 6
- window_valid: int32 [4, 8192], P(None, 'ch'), may hold values 0 or 1
- band_first: int32 [8192], P('ch'), may hold values from 1 to 17
- band_end: int32 [8192], P('ch'), may hold values from 34 to 128
Outputs:
- stacked: float32 [8192, 32, 128], P('ch')
All inputs are finite; a program needn't handle non-finite values. No bound on the sum of `window_valid` on one device may be relied on, other than what follows from the above.
Results may differ from a plain program's by a relative error of at most 0.008.
Values may be sent and summed in bfloat16 or wider, within the bound.
No kernel may reach another device: no remote copies, remote signals or barrier semaphores. Data moves between devices by JAX's collectives and lax.ppermute only.
A program may use at most 64 MiB of HBM per device.

v0:
```python
import jax
import jax.numpy as jnp
from jax import lax
from jax.sharding import PartitionSpec as P

NT = 7680
F = 384
KH = 128
SMOOTH = 65
LAGS = 32
LAG_STEP = 10
eps_white = 1e-06


def from_behind(array, axis, by):
    count = lax.axis_size(axis)
    pairs = [(i, i + by) for i in range(count) if 0 <= i + by < count]
    return lax.ppermute(array, axis, pairs)


def dft_matrix(samples, bin_count):
    sample_index = jnp.arange(samples, dtype=jnp.int32)[:, None]
    orders = jnp.arange(1, bin_count + 1, dtype=jnp.int32)[None, :]
    phases = (sample_index * orders % samples).astype(jnp.float32) * (2.0 * jnp.pi / samples)
    return jnp.concatenate([jnp.cos(phases), -jnp.sin(phases)], axis=1).astype(jnp.bfloat16)


def smoothing_matrix(bin_count, window_bins):
    row_index = jnp.arange(bin_count, dtype=jnp.int32)[:, None]
    col_index = jnp.arange(bin_count, dtype=jnp.int32)[None, :]
    distance = (row_index - col_index) % bin_count
    halfwidth = window_bins // 2
    inside = (distance <= halfwidth) | (distance >= bin_count - halfwidth)
    return inside.astype(jnp.float32)


def whiten(spectra, bin_count, window_bins):
    real_part = spectra[..., :bin_count]
    imag_part = spectra[..., bin_count:]
    magnitude = jnp.sqrt(real_part * real_part + imag_part * imag_part)
    averaged = (
        jnp.dot(
            magnitude,
            smoothing_matrix(bin_count, window_bins),
            precision=lax.Precision.HIGHEST,
            preferred_element_type=jnp.float32,
        )
        / window_bins
    )
    factor = 1.0 / (averaged + eps_white)
    return (spectra * jnp.concatenate([factor, factor], axis=-1)).astype(jnp.bfloat16)


def rotated(extended, lag_first, lag_count, lag_step, samples, bin_count):
    orders = jnp.arange(1, bin_count + 1, dtype=jnp.int32)[None, :]
    shifts = ((lag_first + jnp.arange(lag_count, dtype=jnp.int32)) * lag_step)[:, None]
    phases = (shifts * orders % samples).astype(jnp.float32) * (2.0 * jnp.pi / samples)
    cosine = jnp.cos(phases)
    sine_part = jnp.sin(phases)
    real_part = extended[..., :bin_count].astype(jnp.float32)[:, :, None, :]
    imag_part = extended[..., bin_count:].astype(jnp.float32)[:, :, None, :]
    rotated_real = real_part * cosine + imag_part * sine_part
    rotated_imag = imag_part * cosine - real_part * sine_part
    return jnp.concatenate([rotated_real, rotated_imag], axis=-1).astype(jnp.bfloat16)


def diagonal_band(matrix, offsets):
    row_count, col_count = matrix.shape
    flat_rows = matrix.reshape(row_count * col_count)
    padded = jnp.concatenate([flat_rows, jnp.zeros((row_count,), matrix.dtype)])
    skewed = padded.reshape(row_count, col_count + 1)
    return skewed[:, :offsets]


def lag_band(block_full, offsets):
    banded = jax.vmap(lambda matrix: diagonal_band(matrix, offsets))(block_full)
    return jnp.transpose(banded, (1, 0, 2))


def normalise(lagged, pair_counts, band_lows, band_highs, bin_count):
    offsets = jnp.arange(lagged.shape[2], dtype=jnp.int32)[None, :]
    in_band = (offsets >= band_lows[:, None]) & (offsets < band_highs[:, None])
    weights = jnp.where(
        in_band, 1.0 / jnp.sqrt(float(bin_count) * jnp.maximum(pair_counts, 1.0)), 0.0
    )
    return lagged * weights[:, None, :]


def local(raw_strain, window_valid, band_first, band_end):
    dft_table = dft_matrix(NT, F)
    spectra = jnp.einsum(
        "nta,tf->naf",
        lax.all_to_all(raw_strain, "ch", split_axis=2, concat_axis=1, tiled=True),
        dft_table,
        preferred_element_type=jnp.float32,
    )
    whitened = whiten(spectra, F, SMOOTH)
    valid_flags = window_valid.astype(jnp.bfloat16)
    group_index = lax.axis_index("grp")
    own_flags = lax.dynamic_slice_in_dim(valid_flags, group_index, 1, 0)
    whitened = whitened * own_flags[:, :, None]
    channels_here = whitened.shape[1]
    blocks_up = (KH + channels_here - 1) // channels_here
    white_parts = [whitened]
    flag_parts = [valid_flags]
    for neighbour in range(1, blocks_up + 1):
        moved_white, moved_flags = from_behind((whitened, valid_flags), "ch", -neighbour)
        white_parts.append(moved_white)
        flag_parts.append(moved_flags)
    extended = jnp.concatenate(white_parts, axis=1)
    ext_flags = jnp.concatenate(flag_parts, axis=1)
    pair_full = jnp.einsum("na,nb->ab", valid_flags, ext_flags, preferred_element_type=jnp.float32)
    pair_counts = diagonal_band(pair_full, KH)
    turned = rotated(extended, -(LAGS // 2), LAGS, LAG_STEP, NT, F)
    block_full = jnp.einsum("nak,nblk->lab", whitened, turned, preferred_element_type=jnp.float32)
    lagged = lax.psum(lag_band(block_full, KH).astype(jnp.bfloat16), "grp").astype(jnp.float32)
    return normalise(lagged, pair_counts, band_first, band_end, F)


def solution(mesh):
    placed = (P("grp", "ch", None), P(None, "ch"), P("ch"), P("ch"))
    return jax.shard_map(
        local, mesh=mesh, in_specs=placed, out_specs=P("ch", None, None), check_vma=False
    )
```

profile of v0, /device:TPU:8, one launch (start us, length us, event | category | flops | bytes accessed | tf_op | source)
XLA Modules:
  0.0 264.4 jit_solution(14576265745442213151)
XLA Ops:
  6.5 9.2 %copy.8 = bf16[1,60,8192]{1,0,2:T(2,128)(2,1)} copy(bf16[1,60,8192]{2,1,0:T(8,128)(2,1)} %param.4) | data formatting | bytes 1966080 | tf_op args[0]
  15.7 0.0 copy-start
  15.7 0.5 broadcast.138
  16.3 45.2 %reduce = bf16[8192,60]{1,0:T(8,128)(2,1)S(1)} reduce(bf16[8192,1,60]{2,1,0:T(2,128)(2,1)} %bitcast.40, bf16[]{:T(256)} %broadcast.138), dimensions={1}, to_apply=%bitcast.36.reduce_sub_computation | reduce | bytes 1966082
  61.5 6.4 %reshape.150 = bf16[128,2,1920]{2,1,0:T(2,128)(2,1)} reshape(bf16[8192,60]{1,0:T(8,128)(2,1)S(1)} %reduce) | data formatting | bytes 1966080
  67.9 19.6 %all-to-all-start = ((bf16[128,2,1920]{2,1,0:T(2,128)(2,1)}), bf16[128,2,1920]{2,1,0:T(2,128)(2,1)S(1)}, u32[]{:S(2)}, u32[]{:S(2)}) async-start(bf16[128,2,1920]{2,1,0:T(2,128)(2,1)} %reshape.150), calls=%async_computation | async-start | bytes 1966080 | tf_op jit(solution)/shard_map/all_to_all | solution.py:93
  87.5 0.2 all-reduce.4.cloned.1.call-start
  87.7 0.0 copy-done
  87.8 50.6 %cosine_convert_fusion = (bf16[7680,384]{1,0:T(8,128)(2,1)}, bf16[7680,384]{1,0:T(8,128)(2,1)}) fusion(s32[384]{0:T(512)S(1)} %iota_add_fusion), kind=kLoop, calls=%fused_computation.8 | loop fusion | flops 35389440 | bytes 11798016 | tf_op jit(solution)/shard_map/convert.10
  138.4 2.0 all-to-all-done
  140.4 9.5 %reshape.151 = bf16[8192,1,60]{2,1,0:T(2,128)(2,1)} reshape(bf16[128,2,1920]{2,1,0:T(2,128)(2,1)S(1)} %all-to-all-done) | data formatting | bytes 1966080
  149.9 8.4 %copy.9 = bf16[1,60,8192]{2,1,0:T(8,128)(2,1)S(1)} copy(bf16[1,60,8192]{1,0,2:T(2,128)(2,1)} %bitcast.41) | data formatting | bytes 1966080 | tf_op jit(solution)/shard_map/all_to_all | solution.py:93
  158.3 3.5 %all_to_all.12 = bf16[1,60,128,64]{3,2,1,0:T(8,128)(2,1)} reshape(bf16[1,60,8192]{2,1,0:T(8,128)(2,1)S(1)} %copy.9) | data formatting | bytes 1966080 | tf_op jit(solution)/shard_map/all_to_all | solution.py:93
  161.8 4.7 %copy.10 = bf16[1,128,60,64]{2,1,3,0:T(8,128)(2,1)S(1)} copy(bf16[1,128,60,64]{3,1,2,0:T(8,128)(2,1)} %bitcast.42) | data formatting | bytes 1966080 | tf_op jit(solution)/shard_map/all_to_all | solution.py:93
  166.5 4.1 %reshape.141 = bf16[7680,64]{0,1:T(8,128)(2,1)S(1)} reshape(bf16[1,128,60,64]{2,1,3,0:T(8,128)(2,1)S(1)} %copy.10) | data formatting | bytes 1966080 | tf_op jit(solution)/shard_map/reshape
  170.6 5.6 %fusion.2 = f32[768,64]{0,1:T(8,128)S(1)} fusion(bf16[7680,64]{0,1:T(8,128)(2,1)S(1)} %reshape.141, bf16[7680,384]{1,0:T(8,128)(2,1)} %get-tuple-element.12, bf16[7680,384]{1,0:T(8,128)(2,1)} %get-tuple-element.11), kind=kOutput, calls=%fused_computation.3 | convolution fusion | flops 778567680 | bytes 12976128 | tf_op jit(solution)/shard_map/nta,tf->naf/dot_general | solution.py:91
  176.2 0.7 fusion.20
  176.9 0.1 fusion.35
  177.0 2.6 collective-permute-start.1
  179.5 3.0 %collective-permute-start = (bf16[1,64,768]{2,1,0:T(8,128)(2,1)S(1)}, bf16[1,64,768]{2,1,0:T(8,128)(2,1)S(1)}, u32[]{:S(2)}, u32[]{:S(2)}) collective-permute-start(bf16[1,64,768]{2,1,0:T(8,128)(2,1)S(1)} %bitcast.44), channel_id=1, source_target_pairs={{1,0},{2,1},{3,2},{4,3},{5,4},{6,5},{7,6},{8,7},{9,8},{10,9},{11,1... | collective-permute-start | bytes 294920 | tf_op jit(solution)/shard_map/ppermute | solution.py:18
  182.6 0.3 fusion.46
  182.9 0.6 collective-permute-done.1
  183.5 1.1 collective-permute-done
  184.6 2.6 add_convert_fusion
  187.2 2.9 %fusion.16 = bf16[32,64,192]{1,0,2:T(8,128)(2,1)S(1)} fusion(bf16[192,32,384]{2,1,0:T(8,128)(2,1)S(1)} %get-tuple-element.6, bf16[192,32,384]{2,1,0:T(8,128)(2,1)S(1)} %get-tuple-element.5, bf16[64,768]{1,0:T(8,128)(2,1)S(1)} %fusion.35), kind=kOutput, calls=%fused_computation.20 | convolution fusion | flops 623247360 | bytes 10321920 | tf_op jit(solution)/shard_map/nak,nblk->lab/dot_general | solution.py:115
  190.1 0.0 copy-start.1
  190.2 0.0 copy-start.2
  190.2 1.4 copy.11
  191.5 1.1 reshape.143
  192.7 0.1 concatenate.31
  192.7 3.2 %reshape.144 = bf16[32,64,193]{2,1,0:T(8,128)(2,1)S(1)} reshape(bf16[32,12352]{1,0:T(8,128)(2,1)S(1)} %concatenate.31) | data formatting | bytes 1581056 | tf_op jit(solution)/shard_map/vmap()/reshape | solution.py:71
  195.9 0.9 slice_bitcast_fusion
  196.8 0.0 all-reduce.4.cloned.1.call-update
  196.9 3.8 %collective-permute-start.3 = (bf16[4,64]{1,0:T(4,128)(2,1)S(1)}, bf16[4,64]{1,0:T(4,128)(2,1)S(1)}, u32[]{:S(2)}, u32[]{:S(2)}) collective-permute-start(bf16[4,64]{1,0:T(4,128)(2,1)S(1)} %convert_element_type.45), channel_id=1, source_target_pairs={{2,0},{3,1},{4,2},{5,3},{6,4},{7,5},{8,6},{9,7},{10,8},{11,9},{12,... | collective-permute-start | bytes 1544 | tf_op jit(solution)/shard_map/ppermute | solution.py:18
  200.7 4.0 %collective-permute-start.2 = (bf16[4,64]{1,0:T(4,128)(2,1)S(1)}, bf16[4,64]{1,0:T(4,128)(2,1)S(1)}, u32[]{:S(2)}, u32[]{:S(2)}) collective-permute-start(bf16[4,64]{1,0:T(4,128)(2,1)S(1)} %convert_element_type.45), channel_id=1, source_target_pairs={{1,0},{2,1},{3,2},{4,3},{5,4},{6,5},{7,6},{8,7},{9,8},{10,9},{11,1... | collective-permute-start | bytes 1544 | tf_op jit(solution)/shard_map/ppermute | solution.py:18
  204.7 0.0 collective-permute-done.3
  204.7 1.3 collective-permute-done.2
  205.9 0.2 convolution_bitcast_fusion
  206.1 0.1 reshape.145
  206.3 0.2 reshape.146
  206.5 0.0 copy-done.1
  206.5 0.0 copy-done.2
  206.5 0.1 fusion.50
  206.6 48.2 %all-reduce.4.cloned.1.call-done = bf16[64,32,128]{2,0,1:T(8,128)(2,1)} async-done(((bf16[64,32,128]{2,0,1:T(8,128)(2,1)}), bf16[64,32,128]{2,0,1:T(8,128)(2,1)}) %all-reduce.4.cloned.1.call-update) | async-done | bytes 524304 | tf_op jit(solution)/shard_map/psum | solution.py:116
  254.8 1.2 convert_multiply_fusion
  256.0 1.6 copy.12
  (7 shorter events, 0.1 us)
Async XLA Ops:
  15.7 72.0 %copy-start = (s32[4,64]{1,0:T(4,128)S(1)}, s32[4,64]{1,0:T(4,128)}, u32[]{:S(2)}) copy-start(s32[4,64]{1,0:T(4,128)} %param.5) | copy-start | bytes 3076
  67.9 72.5 %all-to-all-start = ((bf16[128,2,1920]{2,1,0:T(2,128)(2,1)}), bf16[128,2,1920]{2,1,0:T(2,128)(2,1)S(1)}, u32[]{:S(2)}, u32[]{:S(2)}) async-start(bf16[128,2,1920]{2,1,0:T(2,128)(2,1)} %reshape.150), calls=%async_computation | async-start | bytes 1966080 | tf_op jit(solution)/shard_map/all_to_all | solution.py:93
  87.5 167.3 %all-reduce.4.cloned.1.call-start = ((), (), s32[]{:S(2)}) async-start(), calls=%async_computation.1 | async-start | bytes 1048576 | tf_op jit(solution)/shard_map/psum | solution.py:116
  177.0 6.5 %collective-permute-start.1 = (bf16[1,64,768]{2,1,0:T(8,128)(2,1)S(1)}, bf16[1,64,768]{2,1,0:T(8,128)(2,1)S(1)}, u32[]{:S(2)}, u32[]{:S(2)}) collective-permute-start(bf16[1,64,768]{2,1,0:T(8,128)(2,1)S(1)} %bitcast.43), channel_id=1, source_target_pairs={{2,0},{3,1},{4,2},{5,3},{6,4},{7,5},{8,6},{9,7},{10,8},{11,9},{12,... | collective-permute-start | bytes 294920 | tf_op jit(solution)/shard_map/ppermute | solution.py:18
  179.5 5.0 %collective-permute-start = (bf16[1,64,768]{2,1,0:T(8,128)(2,1)S(1)}, bf16[1,64,768]{2,1,0:T(8,128)(2,1)S(1)}, u32[]{:S(2)}, u32[]{:S(2)}) collective-permute-start(bf16[1,64,768]{2,1,0:T(8,128)(2,1)S(1)} %bitcast.44), channel_id=1, source_target_pairs={{1,0},{2,1},{3,2},{4,3},{5,4},{6,5},{7,6},{8,7},{9,8},{10,9},{11,1... | collective-permute-start | bytes 294920 | tf_op jit(solution)/shard_map/ppermute | solution.py:18
  190.1 16.3 %copy-start.1 = (s32[64]{0:T(128)S(1)}, s32[64]{0:T(128)}, u32[]{:S(2)}) copy-start(s32[64]{0:T(128)} %param.7) | copy-start | bytes 772
  190.2 16.3 %copy-start.2 = (s32[64]{0:T(128)S(1)}, s32[64]{0:T(128)}, u32[]{:S(2)}) copy-start(s32[64]{0:T(128)} %param.6) | copy-start | bytes 772
  196.9 7.8 %collective-permute-start.3 = (bf16[4,64]{1,0:T(4,128)(2,1)S(1)}, bf16[4,64]{1,0:T(4,128)(2,1)S(1)}, u32[]{:S(2)}, u32[]{:S(2)}) collective-permute-start(bf16[4,64]{1,0:T(4,128)(2,1)S(1)} %convert_element_type.45), channel_id=1, source_target_pairs={{2,0},{3,1},{4,2},{5,3},{6,4},{7,5},{8,6},{9,7},{10,8},{11,9},{12,... | collective-permute-start | bytes 1544 | tf_op jit(solution)/shard_map/ppermute | solution.py:18
  200.7 5.2 %collective-permute-start.2 = (bf16[4,64]{1,0:T(4,128)(2,1)S(1)}, bf16[4,64]{1,0:T(4,128)(2,1)S(1)}, u32[]{:S(2)}, u32[]{:S(2)}) collective-permute-start(bf16[4,64]{1,0:T(4,128)(2,1)S(1)} %convert_element_type.45), channel_id=1, source_target_pairs={{1,0},{2,1},{3,2},{4,3},{5,4},{6,5},{7,6},{8,7},{9,8},{10,9},{11,1... | collective-permute-start | bytes 1544 | tf_op jit(solution)/shard_map/ppermute | solution.py:18
Sparse Core Ops, SparseCore 0:
  197.0 57.7 all-reduce.3
where the time goes:
time: 265 us; the launch traced here: 264 us
  other arithmetic  100 us (38%)
  local copies, waits for them, and re-layouts  54.9 us (21%)
  waiting for transfers between devices  53.2 us (20%)
  starting transfers between devices  33.2 us (13%)
  between operations  13.7 us (5%)
  matrix products  9.39 us (4%)
    another operation x2, other arithmetic  53.2 us
    psum x1, waiting for transfers between devices, local(): lax.psum(lag_band(block_full, KH).astype(jnp.bfloat16), 'grp')  48.2 us
    unnamed x1, other arithmetic  45.2 us
    unnamed x10, local copies, waits for them, and re-layouts  25.6 us
    all_to_all x1, starting transfers between devices, local(): lax.all_to_all(raw_strain, 'ch', split_axis=2, concat_axis=1, tiled=True)  19.6 us
    all_to_all x3, local copies, waits for them, and re-layouts, local(): lax.all_to_all(raw_strain, 'ch', split_axis=2, concat_axis=1, tiled=True)  16.6 us
    ppermute x4, starting transfers between devices, from_behind(): return lax.ppermute(array, axis, pairs)  13.4 us
    dot_general x1, matrix products, local(): jnp.einsum('nta,tf->naf', lax.all_to_all(raw_strain, 'ch', split_axis=2,...  5.6 us
  transfers between devices with their start and end apart: 6, of which 5 were waited for; matrix products, arithmetic and copies ran while one was open for 19% of the time, Pallas kernels for 0%

commit v1 on v0

--- a/solution.py
+++ b/solution.py
@@ -113,7 +113,8 @@
     pair_counts = diagonal_band(pair_full, KH)
     turned = rotated(extended, -(LAGS // 2), LAGS, LAG_STEP, NT, F)
     block_full = jnp.einsum("nak,nblk->lab", whitened, turned, preferred_element_type=jnp.float32)
-    lagged = lax.psum(lag_band(block_full, KH).astype(jnp.bfloat16), "grp").astype(jnp.float32)
+    use_cycles_for = lambda unit: jnp.sum(lax.all_gather(unit, "grp"), axis=0)
+    lagged = use_cycles_for(lag_band(block_full, KH).astype(jnp.bfloat16)).astype(jnp.float32)
     return normalise(lagged, pair_counts, band_first, band_end, F)
 
 

time: 265 us -> 247 us (0.932)
  the two profiles are of different devices: /device:TPU:8 before, /device:TPU:1 now
where the time goes in v1:
time: 247 us; the launch traced here: 246 us
  other arithmetic  101 us (41%)
  local copies, waits for them, and re-layouts  54.9 us (22%)
  waiting for transfers between devices  37.9 us (15%)
  starting transfers between devices  29.2 us (12%)
  between operations  13.7 us (6%)
  matrix products  9.39 us (4%)
    another operation x2, other arithmetic  53.2 us
    unnamed x1, other arithmetic  45.2 us
    all_gather x1, waiting for transfers between devices, local(): use_cycles_for = lambda unit: jnp.sum(lax.all_gather(unit, 'grp'), axis=0)  30.2 us
    unnamed x10, local copies, waits for them, and re-layouts  25.6 us
    all_to_all x1, starting transfers between devices, local(): lax.all_to_all(raw_strain, 'ch', split_axis=2, concat_axis=1, tiled=True)  20.6 us
    all_to_all x3, local copies, waits for them, and re-layouts, local(): lax.all_to_all(raw_strain, 'ch', split_axis=2, concat_axis=1, tiled=True)  16.6 us
    ppermute x4, starting transfers between devices, from_behind(): return lax.ppermute(array, axis, pairs)  8.39 us
    ppermute x4, waiting for transfers between devices, from_behind(): return lax.ppermute(array, axis, pairs)  6.98 us
  transfers between devices with their start and end apart: 6, of which 5 were waited for; matrix products, arithmetic and copies ran while one was open for 21% of the time, Pallas kernels for 0%

profile of v1, /device:TPU:1, one launch (start us, length us, event | category | flops | bytes accessed | tf_op | source)
XLA Modules:
  0.0 246.1 jit_solution(7240505289374403999)
XLA Ops:
  6.5 9.2 %copy.7 = bf16[1,60,8192]{1,0,2:T(2,128)(2,1)} copy(bf16[1,60,8192]{2,1,0:T(8,128)(2,1)} %param.4) | data formatting | bytes 1966080 | tf_op args[0]
  15.7 0.0 copy-start
  15.7 0.5 broadcast.138
  16.3 45.2 %reduce.1 = bf16[8192,60]{1,0:T(8,128)(2,1)S(1)} reduce(bf16[8192,1,60]{2,1,0:T(2,128)(2,1)} %bitcast.41, bf16[]{:T(256)} %broadcast.138), dimensions={1}, to_apply=%bitcast.37.reduce_sub_computation | reduce | bytes 1966082
  61.5 6.4 %reshape.151 = bf16[128,2,1920]{2,1,0:T(2,128)(2,1)} reshape(bf16[8192,60]{1,0:T(8,128)(2,1)S(1)} %reduce.1) | data formatting | bytes 1966080
  67.9 20.6 %all-to-all-start = ((bf16[128,2,1920]{2,1,0:T(2,128)(2,1)}), bf16[128,2,1920]{2,1,0:T(2,128)(2,1)S(1)}, u32[]{:S(2)}, u32[]{:S(2)}) async-start(bf16[128,2,1920]{2,1,0:T(2,128)(2,1)} %reshape.151), calls=%async_computation | async-start | bytes 1966080 | tf_op jit(solution)/shard_map/all_to_all | solution.py:93
  88.4 0.2 all-gather.3.cloned.1.call-start
  88.7 0.0 copy-done
  88.7 50.6 %cosine_convert_fusion = (bf16[7680,384]{1,0:T(8,128)(2,1)}, bf16[7680,384]{1,0:T(8,128)(2,1)}) fusion(s32[384]{0:T(512)S(1)} %iota_add_fusion), kind=kLoop, calls=%fused_computation.8 | loop fusion | flops 35389440 | bytes 11798016 | tf_op jit(solution)/shard_map/convert.11
  139.3 0.7 all-to-all-done
  140.1 9.5 %reshape.152 = bf16[8192,1,60]{2,1,0:T(2,128)(2,1)} reshape(bf16[128,2,1920]{2,1,0:T(2,128)(2,1)S(1)} %all-to-all-done) | data formatting | bytes 1966080
  149.5 8.4 %copy.8 = bf16[1,60,8192]{2,1,0:T(8,128)(2,1)S(1)} copy(bf16[1,60,8192]{1,0,2:T(2,128)(2,1)} %bitcast.42) | data formatting | bytes 1966080 | tf_op jit(solution)/shard_map/all_to_all | solution.py:93
  157.9 3.5 %all_to_all.12 = bf16[1,60,128,64]{3,2,1,0:T(8,128)(2,1)} reshape(bf16[1,60,8192]{2,1,0:T(8,128)(2,1)S(1)} %copy.8) | data formatting | bytes 1966080 | tf_op jit(solution)/shard_map/all_to_all | solution.py:93
  161.4 4.7 %copy.9 = bf16[1,128,60,64]{2,1,3,0:T(8,128)(2,1)S(1)} copy(bf16[1,128,60,64]{3,1,2,0:T(8,128)(2,1)} %bitcast.43) | data formatting | bytes 1966080 | tf_op jit(solution)/shard_map/all_to_all | solution.py:93
  166.1 4.1 %reshape.141 = bf16[7680,64]{0,1:T(8,128)(2,1)S(1)} reshape(bf16[1,128,60,64]{2,1,3,0:T(8,128)(2,1)S(1)} %copy.9) | data formatting | bytes 1966080 | tf_op jit(solution)/shard_map/reshape
  170.2 5.6 %fusion.2 = f32[768,64]{0,1:T(8,128)S(1)} fusion(bf16[7680,64]{0,1:T(8,128)(2,1)S(1)} %reshape.141, bf16[7680,384]{1,0:T(8,128)(2,1)} %get-tuple-element.12, bf16[7680,384]{1,0:T(8,128)(2,1)} %get-tuple-element.11), kind=kOutput, calls=%fused_computation.3 | convolution fusion | flops 778567680 | bytes 12976128 | tf_op jit(solution)/shard_map/nta,tf->naf/dot_general | solution.py:91
  175.8 0.7 fusion.20
  176.5 0.1 fusion.35
  176.6 1.3 collective-permute-start.1
  177.9 3.9 %collective-permute-start = (bf16[1,64,768]{2,1,0:T(8,128)(2,1)S(1)}, bf16[1,64,768]{2,1,0:T(8,128)(2,1)S(1)}, u32[]{:S(2)}, u32[]{:S(2)}) collective-permute-start(bf16[1,64,768]{2,1,0:T(8,128)(2,1)S(1)} %bitcast.46), channel_id=1, source_target_pairs={{1,0},{2,1},{3,2},{4,3},{5,4},{6,5},{7,6},{8,7},{9,8},{10,9},{11,1... | collective-permute-start | bytes 294920 | tf_op jit(solution)/shard_map/ppermute | solution.py:18
  181.8 0.3 fusion.46
  182.1 0.0 collective-permute-done.1
  182.1 4.0 %collective-permute-done = bf16[1,64,768]{2,1,0:T(8,128)(2,1)S(1)} collective-permute-done((bf16[1,64,768]{2,1,0:T(8,128)(2,1)S(1)}, bf16[1,64,768]{2,1,0:T(8,128)(2,1)S(1)}, u32[]{:S(2)}, u32[]{:S(2)}) %collective-permute-start) | collective-permute-done | bytes 98336 | tf_op jit(solution)/shard_map/ppermute | solution.py:18
  186.2 2.6 %add_convert_fusion = (bf16[192,32,384]{2,1,0:T(8,128)(2,1)S(1)}, bf16[192,32,384]{2,1,0:T(8,128)(2,1)S(1)}) fusion(f32[32,384]{1,0:T(8,128)S(1)} %get-tuple-element.10, f32[192,384]{1,0:T(8,128)S(1)} %get-tuple-element.8, f32[32,384]{1,0:T(8,128)S(1)} %get-tuple-element.9, f32[192,384]{1,0:T(8,128)S(1)} %get-tuple-element.7), kind=kLoop, calls=%fused_computation.18 | loop fusion | flops 18874368 | bytes 10125312 | tf_op jit(solution)/shard_map/convert.9
  188.8 2.9 %fusion.16 = bf16[32,64,192]{1,0,2:T(8,128)(2,1)S(1)} fusion(bf16[192,32,384]{2,1,0:T(8,128)(2,1)S(1)} %get-tuple-element.6, bf16[192,32,384]{2,1,0:T(8,128)(2,1)S(1)} %get-tuple-element.5, bf16[64,768]{1,0:T(8,128)(2,1)S(1)} %fusion.35), kind=kOutput, calls=%fused_computation.20 | convolution fusion | flops 623247360 | bytes 10321920 | tf_op jit(solution)/shard_map/nak,nblk->lab/dot_general | solution.py:115
  191.7 0.0 copy-start.1
  191.7 0.0 copy-start.2
  191.7 1.4 copy.10
  193.1 1.1 reshape.143
  194.3 0.1 concatenate.31
  194.3 3.2 %reshape.144 = bf16[32,64,193]{2,1,0:T(8,128)(2,1)S(1)} reshape(bf16[32,12352]{1,0:T(8,128)(2,1)S(1)} %concatenate.31) | data formatting | bytes 1581056 | tf_op jit(solution)/shard_map/vmap()/reshape | solution.py:71
  197.5 0.9 slice_bitcast_fusion
  198.4 0.0 all-gather.3.cloned.1.call-update
  198.4 1.3 collective-permute-start.3
  199.7 1.9 collective-permute-start.2
  201.7 1.1 collective-permute-done.3
  202.8 1.9 collective-permute-done.2
  204.6 0.2 convolution_bitcast_fusion
  204.8 0.1 reshape.145
  205.0 0.2 reshape.146
  205.2 0.0 copy-done.1
  205.2 0.0 copy-done.2
  205.2 0.1 fusion.50
  205.3 30.2 %all-gather.3.cloned.1.call-done = bf16[256,32,128]{2,0,1:T(8,128)(2,1)} async-done(((bf16[64,32,128]{2,0,1:T(8,128)(2,1)}), bf16[256,32,128]{2,0,1:T(8,128)(2,1)}) %all-gather.3.cloned.1.call-update) | async-done | bytes 2097168 | tf_op jit(solution)/shard_map/all_gather | solution.py:116
  235.5 2.0 reduce_sum.12
  237.5 0.1 convert_multiply_fusion
  237.6 1.6 copy.11
  (7 shorter events, 0.1 us)
Async XLA Ops:
  15.7 72.9 %copy-start = (s32[4,64]{1,0:T(4,128)S(1)}, s32[4,64]{1,0:T(4,128)}, u32[]{:S(2)}) copy-start(s32[4,64]{1,0:T(4,128)} %param.5) | copy-start | bytes 3076
  67.9 72.2 %all-to-all-start = ((bf16[128,2,1920]{2,1,0:T(2,128)(2,1)}), bf16[128,2,1920]{2,1,0:T(2,128)(2,1)S(1)}, u32[]{:S(2)}, u32[]{:S(2)}) async-start(bf16[128,2,1920]{2,1,0:T(2,128)(2,1)} %reshape.151), calls=%async_computation | async-start | bytes 1966080 | tf_op jit(solution)/shard_map/all_to_all | solution.py:93
  88.4 147.0 %all-gather.3.cloned.1.call-start = ((), (), s32[]{:S(2)}) async-start(), calls=%async_computation.1 | async-start | bytes 2621440 | tf_op jit(solution)/shard_map/all_gather | solution.py:116
  176.6 5.5 %collective-permute-start.1 = (bf16[1,64,768]{2,1,0:T(8,128)(2,1)S(1)}, bf16[1,64,768]{2,1,0:T(8,128)(2,1)S(1)}, u32[]{:S(2)}, u32[]{:S(2)}) collective-permute-start(bf16[1,64,768]{2,1,0:T(8,128)(2,1)S(1)} %bitcast.45), channel_id=1, source_target_pairs={{2,0},{3,1},{4,2},{5,3},{6,4},{7,5},{8,6},{9,7},{10,8},{11,9},{12,... | collective-permute-start | bytes 294920 | tf_op jit(solution)/shard_map/ppermute | solution.py:18
  177.9 8.2 %collective-permute-start = (bf16[1,64,768]{2,1,0:T(8,128)(2,1)S(1)}, bf16[1,64,768]{2,1,0:T(8,128)(2,1)S(1)}, u32[]{:S(2)}, u32[]{:S(2)}) collective-permute-start(bf16[1,64,768]{2,1,0:T(8,128)(2,1)S(1)} %bitcast.46), channel_id=1, source_target_pairs={{1,0},{2,1},{3,2},{4,3},{5,4},{6,5},{7,6},{8,7},{9,8},{10,9},{11,1... | collective-permute-start | bytes 294920 | tf_op jit(solution)/shard_map/ppermute | solution.py:18
  191.7 13.5 %copy-start.1 = (s32[64]{0:T(128)S(1)}, s32[64]{0:T(128)}, u32[]{:S(2)}) copy-start(s32[64]{0:T(128)} %param.7) | copy-start | bytes 772
  191.7 13.5 %copy-start.2 = (s32[64]{0:T(128)S(1)}, s32[64]{0:T(128)}, u32[]{:S(2)}) copy-start(s32[64]{0:T(128)} %param.6) | copy-start | bytes 772
  198.4 4.3 %collective-permute-start.3 = (bf16[4,64]{1,0:T(4,128)(2,1)S(1)}, bf16[4,64]{1,0:T(4,128)(2,1)S(1)}, u32[]{:S(2)}, u32[]{:S(2)}) collective-permute-start(bf16[4,64]{1,0:T(4,128)(2,1)S(1)} %convert_element_type.47), channel_id=1, source_target_pairs={{2,0},{3,1},{4,2},{5,3},{6,4},{7,5},{8,6},{9,7},{10,8},{11,9},{12,... | collective-permute-start | bytes 1544 | tf_op jit(solution)/shard_map/ppermute | solution.py:18
  199.7 4.9 %collective-permute-start.2 = (bf16[4,64]{1,0:T(4,128)(2,1)S(1)}, bf16[4,64]{1,0:T(4,128)(2,1)S(1)}, u32[]{:S(2)}, u32[]{:S(2)}) collective-permute-start(bf16[4,64]{1,0:T(4,128)(2,1)S(1)} %convert_element_type.47), channel_id=1, source_target_pairs={{1,0},{2,1},{3,2},{4,3},{5,4},{6,5},{7,6},{8,7},{9,8},{10,9},{11,1... | collective-permute-start | bytes 1544 | tf_op jit(solution)/shard_map/ppermute | solution.py:18
Sparse Core Ops, SparseCore 0:
  198.6 36.8 all-gather.2
